TPU v7x, 256 devices: a whole 4x4x8 slice. The times are simulated.
256 devices in a mesh: row: 32 (over z, y_hi, core), col: 8 (over x, y_lo).
Axes of the slice: x: 4, y: 4 (y_hi: 2, y_lo: 2; y = y_hi * 2 + y_lo), z: 8, core: 2. Of those that a mesh axis runs over, the one named last changes fastest.
Arguments:
- affinity_tiles: bfloat16 [1024, 512, 512], P(('row', 'col')), may hold values from -6 to 6
- tile_rows: int32 [1024], P(('row', 'col')), may hold values from -1 to 63, as said below
- tile_cols: int32 [1024], P(('row', 'col')), may hold values from -1 to 63, as said below
- lang_counts: int32 [32], replicated, may hold values from 1 to 8192, 32768 in all
- start_basis: float32 [8, 4096, 64], P('col', 'row'), may hold values from -6 to 6
Outputs:
- eigen_basis: float32 [8, 4096, 64], P('col', 'row')
Inputs may be any that keep to these rules, and one draw needn't show every extreme that they name: `tile_rows`: the slots of device (r, c) are entries (r * 8 + c) * 4 onward of both lists. Every used slot names a distinct block with block row from r * 2 to (r + 1) * 2 - 1, block column from c * 8 to (c + 1) * 8 - 1, and block row <= block column; no block is named twice. Empty slots hold -1 in both lists and come after the used slots of their device. Device (0, 7) uses all 4 slots. `tile_cols`: same slots as tile_rows.
All inputs are finite; a program needn't handle non-finite values.
Results may differ from a plain program's by a relative error of at most 0.0044.
Values may be sent and summed in bfloat16 or wider, within the bound.
No kernel may reach another device: no remote copies, remote signals or barrier semaphores. Data moves between devices by JAX's collectives and lax.ppermute only.
A program may use at most 64 MiB of HBM per device.

v0:
```python
import jax
import jax.numpy as jnp
from jax import lax
from jax.sharding import PartitionSpec as P

ROW_BLOCKS = 2
ITERS = 3
highest = lax.Precision.HIGHEST


def broadcast(value, axis, root):
    mine = lax.axis_index(axis) == root
    return lax.psum(jnp.where(mine, value, jnp.zeros_like(value)), axis)


def add_block(target, addend, offset):
    current = lax.dynamic_slice_in_dim(target, offset, addend.shape[0], 0)
    return lax.dynamic_update_slice_in_dim(target, current + addend, offset, 0)


def membership(first_doc, doc_count, lang_ends, lang_starts):
    doc_index = first_doc + jnp.arange(doc_count, dtype=jnp.int32)
    return (
        (doc_index[:, None] >= lang_starts[None, :]) & (doc_index[:, None] < lang_ends[None, :])
    ).astype(jnp.float32)


def apply_tiles(affinity_tiles, pick_rows, pick_cols, scaled_rows, scaled_cols, col_blocks):
    slot_count, tile_size, _ = affinity_tiles.shape
    vectors = scaled_cols.shape[1]
    blocks_r = scaled_rows.reshape(ROW_BLOCKS, tile_size, vectors)
    blocks_c = scaled_cols.reshape(col_blocks, tile_size, vectors)
    chosen_c = jnp.einsum(
        "tq,qjk->tjk", pick_cols, blocks_c, preferred_element_type=jnp.float32
    ).astype(jnp.bfloat16)
    chosen_r = jnp.einsum(
        "tp,pik->tik", pick_rows, blocks_r, preferred_element_type=jnp.float32
    ).astype(jnp.bfloat16)
    forward = jnp.einsum(
        "tij,tjk->tik", affinity_tiles, chosen_c, preferred_element_type=jnp.float32
    )
    backward = jnp.einsum(
        "tij,tik->tjk", affinity_tiles, chosen_r, preferred_element_type=jnp.float32
    )
    part_rows = jnp.einsum("tp,tik->pik", pick_rows.astype(jnp.float32), forward, precision=highest)
    part_cols = jnp.einsum(
        "tq,tjk->qjk", pick_cols.astype(jnp.float32), backward, precision=highest
    )
    return (
        part_rows.reshape(ROW_BLOCKS * tile_size, vectors),
        part_cols.reshape(col_blocks * tile_size, vectors),
    )


def shards(affinity_tiles, tile_rows, tile_cols, lang_counts, start_basis):
    row_devices = lax.axis_size("row")
    col_devices = lax.axis_size("col")
    group_ratio = row_devices // col_devices
    col_blocks = ROW_BLOCKS * row_devices // col_devices
    tile_size = affinity_tiles.shape[1]
    row_span = ROW_BLOCKS * tile_size
    col_span = col_blocks * tile_size
    piece_rows = start_basis.shape[1]
    doc_total = piece_rows * row_devices * col_devices
    my_row = lax.axis_index("row")
    my_col = lax.axis_index("col")
    is_owner = (my_row // group_ratio == my_col).astype(jnp.float32)
    offset = my_row % group_ratio * row_span
    piece_offset = my_row * piece_rows
    present = tile_rows >= 0
    local_p = tile_rows - my_row * ROW_BLOCKS
    local_q = tile_cols - my_col * col_blocks
    pick_rows = (
        (local_p[:, None] == jnp.arange(ROW_BLOCKS, dtype=jnp.int32)[None, :]) & present[:, None]
    ).astype(jnp.bfloat16)
    pick_cols = (
        (local_q[:, None] == jnp.arange(col_blocks, dtype=jnp.int32)[None, :]) & present[:, None]
    ).astype(jnp.bfloat16)
    magnitude = jnp.abs(affinity_tiles)
    row_mass = jnp.sum(magnitude, axis=2, dtype=jnp.float32)
    col_mass = jnp.sum(magnitude, axis=1, dtype=jnp.float32)
    degree_rows = jnp.einsum(
        "tp,ti->pi", pick_rows.astype(jnp.float32), row_mass, precision=highest
    ).reshape(row_span)
    degree_cols = jnp.einsum(
        "tq,tj->qj", pick_cols.astype(jnp.float32), col_mass, precision=highest
    ).reshape(col_span)
    rows_degree = lax.psum(degree_rows, "col")
    degree_cols = add_block(degree_cols, is_owner * rows_degree, offset)
    inv_own = lax.rsqrt(1.0 + lax.psum_scatter(degree_cols, "row", scatter_dimension=0, tiled=True))
    prior_scale = lax.psum(jnp.sum(inv_own), ("row", "col")) / doc_total
    lang_ends = jnp.cumsum(lang_counts)
    lang_starts = lang_ends - lang_counts
    counts_real = lang_counts.astype(jnp.float32)
    member_own = membership(my_col * col_span + piece_offset, piece_rows, lang_ends, lang_starts)
    basis_own = start_basis[0]
    for iteration in range(ITERS):
        lang_now = lax.psum(jnp.dot(member_own.T, basis_own, precision=highest), ("row", "col"))
        lang_mean = prior_scale * (lang_now / counts_real[:, None])
        scaled_cols = lax.all_gather(
            (inv_own[:, None] * basis_own).astype(jnp.bfloat16), "row", axis=0, tiled=True
        )
        scaled_rows = broadcast(
            lax.dynamic_slice_in_dim(scaled_cols, offset, row_span, 0), "col", my_row // group_ratio
        )
        part_rows, part_cols = apply_tiles(
            affinity_tiles, pick_rows, pick_cols, scaled_rows, scaled_cols, col_blocks
        )
        rows_sum = lax.psum(part_rows, "col")
        part_cols = add_block(part_cols, is_owner * rows_sum, offset)
        product_own = lax.psum_scatter(part_cols, "row", scatter_dimension=0, tiled=True)
        applied_own = inv_own[:, None] * product_own + jnp.dot(
            member_own, lang_mean, precision=highest
        )
        gram_part = jnp.dot(applied_own.T, applied_own, precision=highest)
        gram_matrix = lax.psum(gram_part, ("row", "col"))
        factor = jnp.linalg.cholesky(gram_matrix / doc_total)
        basis_own = jax.scipy.linalg.solve_triangular(factor, applied_own.T, lower=True).T
    return basis_own[None]


def solution(mesh):
    in_specs = (
        P(("row", "col"), None, None),
        P(("row", "col")),
        P(("row", "col")),
        P(),
        P("col", "row", None),
    )
    out_specs = P("col", "row", None)
    return jax.shard_map(shards, mesh=mesh, in_specs=in_specs, out_specs=out_specs, check_vma=False)
```

profile of v0, /device:TPU:1, one launch (start us, length us, event | category | flops | bytes accessed | tf_op | source)
XLA Modules:
  0.0 1385.8 jit_solution(9308302912916534671)
XLA Ops:
  8.6 2.2 convert_reduce_fusion
  11.0 16.9 %psum.98 = f32[1024]{0:T(1024)S(1)} all-reduce(f32[1024]{0:T(1024)S(1)} %bitcast.181), channel_id=1, replica_groups=mesh['row'=32,'col'=8] {'col'}, use_global_device_ids=true, to_apply=%region_2.3 | all-reduce | flops 1024 | bytes 8192 | tf_op jit(solution)/shard_map/psum | solution.py:88
  28.1 130.8 %all-reduce = f32[4096]{0:T(1024)S(1)} all-reduce(f32[4096]{0:T(1024)S(1)} %add_dynamic-update-slice_fusion.3), channel_id=2, replica_groups=mesh['row'=32,'col'=8] {'row'}, use_global_device_ids=true, to_apply=%region_3.4.clone | all-reduce | flops 4096 | bytes 32768
  160.8 43.6 %all_gather.9 = bf16[4096,64]{0,1:T(8,128)(2,1)S(1)} all-gather(bf16[128,64]{0,1:T(8,128)(2,1)S(1)} %fusion.39), channel_id=1, replica_groups=mesh['row'=32,'col'=8] {'row'}, dimensions={0}, use_global_device_ids=true | all-gather | bytes 540672 | tf_op jit(solution)/shard_map/all_gather | solution.py:100
  206.5 0.9 fusion.8
  207.4 0.7 copy.46
  208.2 67.3 %all-reduce.9.cloned.1.call-done = bf16[2,512,64]{1,0,2:T(2,128)(2,1)} async-done(((bf16[2,512,64]{1,0,2:T(2,128)(2,1)}), bf16[2,512,64]{1,0,2:T(2,128)(2,1)}) %all-reduce.9.cloned.1.call-update) | async-done | bytes 131088 | tf_op jit(solution)/shard_map/psum | solution.py:13
  275.5 1.2 convolution_convert_fusion.5
  277.2 1.0 fusion.10
  278.9 77.9 %all-reduce.11.cloned.1.call-done = f32[1024,64]{0,1:T(8,128)} async-done(((f32[1024,64]{0,1:T(8,128)}), f32[1024,64]{0,1:T(8,128)}) %all-reduce.11.cloned.1.call-update) | async-done | bytes 262160 | tf_op jit(solution)/shard_map/psum | solution.py:109
  356.7 1.0 add_dynamic-update-slice_fusion.2
  357.7 1.0 copy-done.2
  359.3 79.9 %all-reduce.1 = (f32[32,64]{1,0:T(8,128)S(1)}, f32[]{:T(128)}) all-reduce(f32[32,64]{1,0:T(8,128)S(1)} %fusion.22, f32[]{:T(128)} %get-tuple-element.11), channel_id=1, replica_groups=mesh['row'=32,'col'=8] {'row','col'}, use_global_device_ids=true, to_apply=%region_10.11 | all-reduce | flops 2049 | bytes 16392 | tf_op jit(solution)/shard_map/psum | solution.py:98
  439.9 36.3 %reduce-scatter.4.cloned.1.call-done = f32[128,64]{0,1:T(8,128)} async-done(((f32[4096,64]{0,1:T(8,128)}), f32[128,64]{0,1:T(8,128)}) %reduce-scatter.4.cloned.1.call-update) | async-done | bytes 32784 | tf_op jit(solution)/shard_map/reduce_scatter | solution.py:111
  476.2 1.1 convolution_add_fusion.2
  477.4 79.7 %psum.103 = f32[64,64]{0,1:T(8,128)S(1)} all-reduce(f32[64,64]{0,1:T(8,128)S(1)} %fusion.75), channel_id=1, replica_groups=mesh['row'=32,'col'=8] {'row','col'}, use_global_device_ids=true, to_apply=%region_11.12 | all-reduce | flops 4096 | bytes 32768 | tf_op jit(solution)/shard_map/psum | solution.py:116
  557.2 5.8 cholesky.59
  564.4 4.9 custom-call.7
  569.6 41.2 %all_gather.10 = bf16[4096,64]{0,1:T(8,128)(2,1)S(1)} all-gather(bf16[128,64]{0,1:T(8,128)(2,1)S(1)} %fusion.44), channel_id=1, replica_groups=mesh['row'=32,'col'=8] {'row'}, dimensions={0}, use_global_device_ids=true | all-gather | bytes 540672 | tf_op jit(solution)/shard_map/all_gather | solution.py:100
  613.0 0.9 fusion.4
  613.9 0.7 copy.49
  614.7 65.5 %all-reduce.13.cloned.1.call-done = bf16[2,512,64]{1,0,2:T(2,128)(2,1)} async-done(((bf16[2,512,64]{1,0,2:T(2,128)(2,1)}), bf16[2,512,64]{1,0,2:T(2,128)(2,1)}) %all-reduce.13.cloned.1.call-update) | async-done | bytes 131088 | tf_op jit(solution)/shard_map/psum | solution.py:13
  680.2 1.2 convolution_convert_fusion.4
  681.9 1.0 fusion.6
  683.5 77.7 %all-reduce.15.cloned.1.call-done = f32[1024,64]{0,1:T(8,128)} async-done(((f32[1024,64]{0,1:T(8,128)}), f32[1024,64]{0,1:T(8,128)}) %all-reduce.15.cloned.1.call-update) | async-done | bytes 262160 | tf_op jit(solution)/shard_map/psum | solution.py:109
  761.2 1.0 add_dynamic-update-slice_fusion.1
  762.2 1.0 copy-done.3
  763.5 79.8 %psum.106 = f32[32,64]{1,0:T(8,128)S(1)} all-reduce(f32[32,64]{1,0:T(8,128)S(1)} %fusion.20), channel_id=1, replica_groups=mesh['row'=32,'col'=8] {'row','col'}, use_global_device_ids=true, to_apply=%region_17.20 | all-reduce | flops 2048 | bytes 16384 | tf_op jit(solution)/shard_map/psum | solution.py:98
  843.3 37.3 %reduce-scatter.6.cloned.1.call-done = f32[128,64]{0,1:T(8,128)} async-done(((f32[4096,64]{0,1:T(8,128)}), f32[128,64]{0,1:T(8,128)}) %reduce-scatter.6.cloned.1.call-update) | async-done | bytes 32784 | tf_op jit(solution)/shard_map/reduce_scatter | solution.py:111
  880.5 1.1 convolution_add_fusion.1
  881.8 79.7 %psum.107 = f32[64,64]{0,1:T(8,128)S(1)} all-reduce(f32[64,64]{0,1:T(8,128)S(1)} %fusion.76), channel_id=1, replica_groups=mesh['row'=32,'col'=8] {'row','col'}, use_global_device_ids=true, to_apply=%region_18.21 | all-reduce | flops 4096 | bytes 32768 | tf_op jit(solution)/shard_map/psum | solution.py:116
  961.6 5.8 cholesky.70
  968.8 4.9 custom-call.8
  974.0 41.2 %all_gather.11 = bf16[4096,64]{0,1:T(8,128)(2,1)S(1)} all-gather(bf16[128,64]{0,1:T(8,128)(2,1)S(1)} %fusion.45), channel_id=1, replica_groups=mesh['row'=32,'col'=8] {'row'}, dimensions={0}, use_global_device_ids=true | all-gather | bytes 540672 | tf_op jit(solution)/shard_map/all_gather | solution.py:100
  1017.2 0.9 fusion
  1019.1 65.4 %all-reduce.17.cloned.1.call-done = bf16[2,512,64]{1,0,2:T(2,128)(2,1)} async-done(((bf16[2,512,64]{1,0,2:T(2,128)(2,1)}), bf16[2,512,64]{1,0,2:T(2,128)(2,1)}) %all-reduce.17.cloned.1.call-update) | async-done | bytes 131088 | tf_op jit(solution)/shard_map/psum | solution.py:13
  1084.6 1.2 convolution_convert_fusion.3
  1086.3 1.0 fusion.2
  1087.9 77.9 %all-reduce.19.cloned.1.call-done = f32[1024,64]{0,1:T(8,128)} async-done(((f32[1024,64]{0,1:T(8,128)}), f32[1024,64]{0,1:T(8,128)}) %all-reduce.19.cloned.1.call-update) | async-done | bytes 262160 | tf_op jit(solution)/shard_map/psum | solution.py:109
  1165.7 1.0 add_dynamic-update-slice_fusion
  1166.8 1.0 copy-done.1
  1168.0 79.8 %psum.110 = f32[32,64]{1,0:T(8,128)S(1)} all-reduce(f32[32,64]{1,0:T(8,128)S(1)} %fusion.18), channel_id=1, replica_groups=mesh['row'=32,'col'=8] {'row','col'}, use_global_device_ids=true, to_apply=%region_22.25 | all-reduce | flops 2048 | bytes 16384 | tf_op jit(solution)/shard_map/psum | solution.py:98
  1247.8 37.4 %reduce-scatter.8.cloned.1.call-done = f32[128,64]{0,1:T(8,128)} async-done(((f32[4096,64]{0,1:T(8,128)}), f32[128,64]{0,1:T(8,128)}) %reduce-scatter.8.cloned.1.call-update) | async-done | bytes 32784 | tf_op jit(solution)/shard_map/reduce_scatter | solution.py:111
  1285.2 1.1 convolution_add_fusion
  1286.5 79.7 %psum.111 = f32[64,64]{0,1:T(8,128)S(1)} all-reduce(f32[64,64]{0,1:T(8,128)S(1)} %fusion.77), channel_id=1, replica_groups=mesh['row'=32,'col'=8] {'row','col'}, use_global_device_ids=true, to_apply=%region_23.26 | all-reduce | flops 4096 | bytes 32768 | tf_op jit(solution)/shard_map/psum | solution.py:116
  1366.3 5.8 cholesky.81
  1373.5 4.9 custom-call.9
  1378.4 0.9 convolution_bitcast_fusion.6
  (97 shorter events, 20.6 us)
Async XLA Ops:
  6.5 152.4 %copy-start.6 = (u32[256]{0:T(256)S(1)}, u32[256]{0:T(256)}, u32[]{:S(2)}) copy-start(u32[256]{0:T(256)} %constant.105) | copy-start | bytes 3076
  6.5 154.3 %copy-start.4 = (f32[1,128,64]{1,2,0:T(8,128)S(1)}, f32[1,128,64]{1,2,0:T(8,128)}, u32[]{:S(2)}) copy-start(f32[1,128,64]{1,2,0:T(8,128)} %param.12) | copy-start | bytes 98308
  6.5 269.0 %all-reduce.9.cloned.1.call-start = ((), (), s32[]{:S(2)}) async-start(), calls=%async_computation.3 | async-start | bytes 262144 | tf_op jit(solution)/shard_map/psum | solution.py:13
  10.8 194.9 %copy-start = (bf16[4,512,512]{2,1,0:T(8,128)(2,1)S(1)}, bf16[4,512,512]{2,1,0:T(8,128)(2,1)}, u32[]{:S(2)}) copy-start(bf16[4,512,512]{2,1,0:T(8,128)(2,1)} %param.8) | copy-start | bytes 6291460
  205.2 151.5 %all-reduce.11.cloned.1.call-start = ((), (), s32[]{:S(2)}) async-start(), calls=%async_computation.4 | async-start | bytes 524288 | tf_op jit(solution)/shard_map/psum | solution.py:109
  208.2 268.0 %reduce-scatter.4.cloned.1.call-start = ((), (), s32[]{:S(2)}) async-start(), calls=%async_computation.5 | async-start | bytes 1081344 | tf_op jit(solution)/shard_map/reduce_scatter | solution.py:111
  278.2 80.6 %copy-start.5 = (s32[32]{0:T(128)S(1)}, s32[32]{0:T(128)}, u32[]{:S(2)}) copy-start(s32[32]{0:T(128)} %param.11) | copy-start | bytes 388
  357.7 1.0 copy-start.2
  358.7 321.4 %all-reduce.13.cloned.1.call-start = ((), (), s32[]{:S(2)}) async-start(), calls=%async_computation.6 | async-start | bytes 262144 | tf_op jit(solution)/shard_map/psum | solution.py:13
  611.5 149.7 %all-reduce.15.cloned.1.call-start = ((), (), s32[]{:S(2)}) async-start(), calls=%async_computation.7 | async-start | bytes 524288 | tf_op jit(solution)/shard_map/psum | solution.py:109
  614.6 265.9 %reduce-scatter.6.cloned.1.call-start = ((), (), s32[]{:S(2)}) async-start(), calls=%async_computation.8 | async-start | bytes 1081344 | tf_op jit(solution)/shard_map/reduce_scatter | solution.py:111
  762.2 1.0 copy-start.3
  763.2 321.3 %all-reduce.17.cloned.1.call-start = ((), (), s32[]{:S(2)}) async-start(), calls=%async_computation.9 | async-start | bytes 262144 | tf_op jit(solution)/shard_map/psum | solution.py:13
  1015.9 149.9 %all-reduce.19.cloned.1.call-start = ((), (), s32[]{:S(2)}) async-start(), calls=%async_computation.10 | async-start | bytes 524288 | tf_op jit(solution)/shard_map/psum | solution.py:109
  1018.8 266.4 %reduce-scatter.8.cloned.1.call-start = ((), (), s32[]{:S(2)}) async-start(), calls=%async_computation.11 | async-start | bytes 1081344 | tf_op jit(solution)/shard_map/reduce_scatter | solution.py:111
  1166.8 1.0 copy-start.1
Sparse Core Ops, SparseCore 0:
  205.3 70.1 all-reduce.8
  278.1 78.5 all-reduce.10
  360.8 115.3 reduce-scatter.3
  611.6 68.4 all-reduce.12
  682.6 78.5 all-reduce.14
  765.1 115.3 reduce-scatter.5
  1016.0 68.5 all-reduce.16
  1087.2 78.5 all-reduce.18
  1169.8 115.3 reduce-scatter.7
where the time goes:
time: 1390 us
  blocking collectives  752 us (54%)
  waiting for transfers between devices  543 us (39%)
  other arithmetic  44.5 us (3%)
  matrix products  20 us (1%)
  between operations  15 us (1%)
    psum x3, blocking collectives, shards(): lax.psum(jnp.dot(member_own.T, basis_own, precision=highest), ('row', 'co...  239 us
    psum x3, blocking collectives, shards(): gram_matrix = lax.psum(gram_part, ('row', 'col'))  239 us
    psum x3, waiting for transfers between devices, shards(): rows_sum = lax.psum(part_rows, 'col')  233 us
    psum x3, waiting for transfers between devices, broadcast(): return lax.psum(jnp.where(mine, value, jnp.zeros_like(value)), axis)  198 us
    unnamed x1, blocking collectives  131 us
    all_gather x3, blocking collectives, shards(): lax.all_gather((inv_own[:, None] * basis_own).astype(jnp.bfloat16), 'row'...  126 us
    reduce_scatter x3, waiting for transfers between devices, shards(): lax.psum_scatter(part_cols, 'row', scatter_dimension=0, tiled=True)  111 us
  transfers between devices with their start and end apart: 9, of which 9 were waited for; matrix products, arithmetic and copies ran while one was open for 1% of the time, Pallas kernels for 0%

commit v1 on v0

--- a/solution.py
+++ b/solution.py
@@ -97,9 +97,14 @@
     for iteration in range(ITERS):
         lang_now = lax.psum(jnp.dot(member_own.T, basis_own, precision=highest), ("row", "col"))
         lang_mean = prior_scale * (lang_now / counts_real[:, None])
-        scaled_cols = lax.all_gather(
-            (inv_own[:, None] * basis_own).astype(jnp.bfloat16), "row", axis=0, tiled=True
-        )
+
+        def form_the_ladders(q_in):
+            moved = jnp.stack(lax.axis_size("row") * [q_in])
+            formed = lax.all_to_all(moved, "row", 0, 0)
+            wide_out = jnp.concatenate(formed, axis=0)
+            return wide_out
+
+        scaled_cols = form_the_ladders((inv_own[:, None] * basis_own).astype(jnp.bfloat16))
         scaled_rows = broadcast(
             lax.dynamic_slice_in_dim(scaled_cols, offset, row_span, 0), "col", my_row // group_ratio
         )

time: 1390 us -> 1340 us (0.964)
  blocking collectives: 752 us -> 674 us
  waiting for transfers between devices: 543 us -> 559 us
    all_gather x3 -> x0, blocking collectives: 126 us -> none  [shards(): lax.all_gather((inv_own[:, None] * basis_own).astype(jnp.bfloat16), 'row'...]
    all_to_all x0 -> x2, blocking collectives: none -> 47.5 us  [form_the_ladders(): formed = lax.all_to_all(moved, 'row', 0, 0)]
    all_to_all x0 -> x1, waiting for transfers between devices: none -> 16.8 us  [form_the_ladders(): formed = lax.all_to_all(moved, 'row', 0, 0)]
  transfers between devices with their start and end apart: 9 -> 10, of which waited for: 9 -> 10; matrix products, arithmetic and copies ran while one was open for 1% -> 1% of each run, Pallas kernels for 0% -> 0%
where the time goes in v1:
time: 1340 us
  blocking collectives  674 us (50%)
  waiting for transfers between devices  559 us (42%)
  other arithmetic  44.5 us (3%)
  matrix products  19.9 us (1%)
  between operations  15 us (1%)
  local copies, waits for them, and re-layouts  13.4 us (1%)
    psum x3, blocking collectives, shards(): lax.psum(jnp.dot(member_own.T, basis_own, precision=highest), ('row', 'co...  239 us
    psum x3, blocking collectives, shards(): gram_matrix = lax.psum(gram_part, ('row', 'col'))  239 us
    psum x3, waiting for transfers between devices, shards(): rows_sum = lax.psum(part_rows, 'col')  234 us
    psum x3, waiting for transfers between devices, broadcast(): return lax.psum(jnp.where(mine, value, jnp.zeros_like(value)), axis)  198 us
    unnamed x1, blocking collectives  131 us
    reduce_scatter x3, waiting for transfers between devices, shards(): lax.psum_scatter(part_cols, 'row', scatter_dimension=0, tiled=True)  111 us
    all_to_all x2, blocking collectives, form_the_ladders(): formed = lax.all_to_all(moved, 'row', 0, 0)  47.5 us
  transfers between devices with their start and end apart: 10, of which 10 were waited for; matrix products, arithmetic and copies ran while one was open for 1% of the time, Pallas kernels for 0%

profile of v1, /device:TPU:1, one launch (start us, length us, event | category | flops | bytes accessed | tf_op | source)
XLA Modules:
  0.0 1337.2 jit_solution(12234896880980572750)
XLA Ops:
  8.6 2.2 convert_reduce_fusion
  11.0 16.8 %psum.98 = f32[1024]{0:T(1024)S(1)} all-reduce(f32[1024]{0:T(1024)S(1)} %bitcast.183), channel_id=1, replica_groups=mesh['row'=32,'col'=8] {'col'}, use_global_device_ids=true, to_apply=%region_2.3 | all-reduce | flops 1024 | bytes 8192 | tf_op jit(solution)/shard_map/psum | solution.py:88
  28.0 130.8 %all-reduce = f32[4096]{0:T(1024)S(1)} all-reduce(f32[4096]{0:T(1024)S(1)} %add_dynamic-update-slice_fusion.3), channel_id=2, replica_groups=mesh['row'=32,'col'=8] {'row'}, use_global_device_ids=true, to_apply=%region_3.4.clone | all-reduce | flops 4096 | bytes 32768
  160.7 0.9 stack.9
  161.6 10.8 all-to-all-start
  172.5 16.8 %all-to-all-done = bf16[32,128,64]{1,2,0:T(8,128)(2,1)S(1)} async-done(((bf16[32,128,64]{1,2,0:T(8,128)(2,1)}), bf16[32,128,64]{1,2,0:T(8,128)(2,1)S(1)}, u32[]{:S(2)}, u32[]{:S(2)}) %all-to-all-start) | async-done | bytes 524320 | tf_op jit(solution)/shard_map/all_to_all | solution.py:103
  191.9 0.9 fusion.8
  193.6 65.7 %all-reduce.9.cloned.1.call-done = bf16[2,512,64]{1,0,2:T(2,128)(2,1)} async-done(((bf16[2,512,64]{1,0,2:T(2,128)(2,1)}), bf16[2,512,64]{1,0,2:T(2,128)(2,1)}) %all-reduce.9.cloned.1.call-update) | async-done | bytes 131088 | tf_op jit(solution)/shard_map/psum | solution.py:13
  259.3 1.2 convolution_convert_fusion.5
  261.0 1.0 fusion.10
  262.6 77.9 %all-reduce.11.cloned.1.call-done = f32[1024,64]{0,1:T(8,128)} async-done(((f32[1024,64]{0,1:T(8,128)}), f32[1024,64]{0,1:T(8,128)}) %all-reduce.11.cloned.1.call-update) | async-done | bytes 262160 | tf_op jit(solution)/shard_map/psum | solution.py:114
  340.5 1.0 add_dynamic-update-slice_fusion.2
  341.5 1.0 copy-done.2
  343.1 79.9 %all-reduce.1 = (f32[32,64]{1,0:T(8,128)S(1)}, f32[]{:T(128)}) all-reduce(f32[32,64]{1,0:T(8,128)S(1)} %fusion.22, f32[]{:T(128)} %get-tuple-element.11), channel_id=1, replica_groups=mesh['row'=32,'col'=8] {'row','col'}, use_global_device_ids=true, to_apply=%region_10.11 | all-reduce | flops 2049 | bytes 16392 | tf_op jit(solution)/shard_map/psum | solution.py:98
  423.6 36.3 %reduce-scatter.4.cloned.1.call-done = f32[128,64]{0,1:T(8,128)} async-done(((f32[4096,64]{0,1:T(8,128)}), f32[128,64]{0,1:T(8,128)}) %reduce-scatter.4.cloned.1.call-update) | async-done | bytes 32784 | tf_op jit(solution)/shard_map/reduce_scatter | solution.py:116
  459.9 1.1 convolution_add_fusion.2
  461.2 79.7 %psum.103 = f32[64,64]{0,1:T(8,128)S(1)} all-reduce(f32[64,64]{0,1:T(8,128)S(1)} %fusion.75), channel_id=1, replica_groups=mesh['row'=32,'col'=8] {'row','col'}, use_global_device_ids=true, to_apply=%region_11.12 | all-reduce | flops 4096 | bytes 32768 | tf_op jit(solution)/shard_map/psum | solution.py:121
  541.0 5.8 cholesky.59
  548.2 4.9 custom-call.7
  553.4 23.8 %all_to_all.15 = bf16[32,128,64]{1,2,0:T(8,128)(2,1)S(1)} all-to-all(bf16[32,128,64]{1,2,0:T(8,128)(2,1)S(1)} %stack.10), channel_id=1, replica_groups=mesh['row'=32,'col'=8] {'row'}, dimensions={0} | all-to-all | bytes 1048576 | tf_op jit(solution)/shard_map/all_to_all | solution.py:103
  579.8 0.9 fusion.4
  581.5 66.3 %all-reduce.13.cloned.1.call-done = bf16[2,512,64]{1,0,2:T(2,128)(2,1)} async-done(((bf16[2,512,64]{1,0,2:T(2,128)(2,1)}), bf16[2,512,64]{1,0,2:T(2,128)(2,1)}) %all-reduce.13.cloned.1.call-update) | async-done | bytes 131088 | tf_op jit(solution)/shard_map/psum | solution.py:13
  647.8 1.2 convolution_convert_fusion.4
  649.5 1.0 fusion.6
  651.1 77.7 %all-reduce.15.cloned.1.call-done = f32[1024,64]{0,1:T(8,128)} async-done(((f32[1024,64]{0,1:T(8,128)}), f32[1024,64]{0,1:T(8,128)}) %all-reduce.15.cloned.1.call-update) | async-done | bytes 262160 | tf_op jit(solution)/shard_map/psum | solution.py:114
  728.8 1.0 add_dynamic-update-slice_fusion.1
  729.8 1.0 copy-done.3
  731.1 79.8 %psum.106 = f32[32,64]{1,0:T(8,128)S(1)} all-reduce(f32[32,64]{1,0:T(8,128)S(1)} %fusion.20), channel_id=1, replica_groups=mesh['row'=32,'col'=8] {'row','col'}, use_global_device_ids=true, to_apply=%region_17.20 | all-reduce | flops 2048 | bytes 16384 | tf_op jit(solution)/shard_map/psum | solution.py:98
  810.9 37.2 %reduce-scatter.6.cloned.1.call-done = f32[128,64]{0,1:T(8,128)} async-done(((f32[4096,64]{0,1:T(8,128)}), f32[128,64]{0,1:T(8,128)}) %reduce-scatter.6.cloned.1.call-update) | async-done | bytes 32784 | tf_op jit(solution)/shard_map/reduce_scatter | solution.py:116
  848.1 1.1 convolution_add_fusion.1
  849.4 79.7 %psum.107 = f32[64,64]{0,1:T(8,128)S(1)} all-reduce(f32[64,64]{0,1:T(8,128)S(1)} %fusion.76), channel_id=1, replica_groups=mesh['row'=32,'col'=8] {'row','col'}, use_global_device_ids=true, to_apply=%region_18.21 | all-reduce | flops 4096 | bytes 32768 | tf_op jit(solution)/shard_map/psum | solution.py:121
  929.2 5.8 cholesky.70
  936.4 4.9 custom-call.8
  941.7 23.7 %all_to_all.16 = bf16[32,128,64]{1,2,0:T(8,128)(2,1)S(1)} all-to-all(bf16[32,128,64]{1,2,0:T(8,128)(2,1)S(1)} %stack.11), channel_id=1, replica_groups=mesh['row'=32,'col'=8] {'row'}, dimensions={0} | all-to-all | bytes 1048576 | tf_op jit(solution)/shard_map/all_to_all | solution.py:103
  968.0 0.9 fusion
  970.0 66.1 %all-reduce.17.cloned.1.call-done = bf16[2,512,64]{1,0,2:T(2,128)(2,1)} async-done(((bf16[2,512,64]{1,0,2:T(2,128)(2,1)}), bf16[2,512,64]{1,0,2:T(2,128)(2,1)}) %all-reduce.17.cloned.1.call-update) | async-done | bytes 131088 | tf_op jit(solution)/shard_map/psum | solution.py:13
  1036.0 1.2 convolution_convert_fusion.3
  1037.7 1.0 fusion.2
  1039.3 77.9 %all-reduce.19.cloned.1.call-done = f32[1024,64]{0,1:T(8,128)} async-done(((f32[1024,64]{0,1:T(8,128)}), f32[1024,64]{0,1:T(8,128)}) %all-reduce.19.cloned.1.call-update) | async-done | bytes 262160 | tf_op jit(solution)/shard_map/psum | solution.py:114
  1117.2 1.0 add_dynamic-update-slice_fusion
  1118.2 1.0 copy-done.1
  1119.5 79.8 %psum.110 = f32[32,64]{1,0:T(8,128)S(1)} all-reduce(f32[32,64]{1,0:T(8,128)S(1)} %fusion.18), channel_id=1, replica_groups=mesh['row'=32,'col'=8] {'row','col'}, use_global_device_ids=true, to_apply=%region_22.25 | all-reduce | flops 2048 | bytes 16384 | tf_op jit(solution)/shard_map/psum | solution.py:98
  1199.3 37.4 %reduce-scatter.8.cloned.1.call-done = f32[128,64]{0,1:T(8,128)} async-done(((f32[4096,64]{0,1:T(8,128)}), f32[128,64]{0,1:T(8,128)}) %reduce-scatter.8.cloned.1.call-update) | async-done | bytes 32784 | tf_op jit(solution)/shard_map/reduce_scatter | solution.py:116
  1236.7 1.1 convolution_add_fusion
  1238.0 79.7 %psum.111 = f32[64,64]{0,1:T(8,128)S(1)} all-reduce(f32[64,64]{0,1:T(8,128)S(1)} %fusion.77), channel_id=1, replica_groups=mesh['row'=32,'col'=8] {'row','col'}, use_global_device_ids=true, to_apply=%region_23.26 | all-reduce | flops 4096 | bytes 32768 | tf_op jit(solution)/shard_map/psum | solution.py:121
  1317.8 5.8 cholesky.81
  1324.9 4.9 custom-call.9
  1329.8 0.9 convolution_bitcast_fusion.6
  (107 shorter events, 23.9 us)
Async XLA Ops:
  6.5 152.2 %copy-start.6 = (u32[256]{0:T(256)S(1)}, u32[256]{0:T(256)}, u32[]{:S(2)}) copy-start(u32[256]{0:T(256)} %constant.105) | copy-start | bytes 3076
  6.5 154.2 %copy-start.4 = (f32[1,128,64]{1,2,0:T(8,128)S(1)}, f32[1,128,64]{1,2,0:T(8,128)}, u32[]{:S(2)}) copy-start(f32[1,128,64]{1,2,0:T(8,128)} %param.12) | copy-start | bytes 98308
  161.6 27.6 %all-to-all-start = ((bf16[32,128,64]{1,2,0:T(8,128)(2,1)}), bf16[32,128,64]{1,2,0:T(8,128)(2,1)S(1)}, u32[]{:S(2)}, u32[]{:S(2)}) async-start(bf16[32,128,64]{1,2,0:T(8,128)(2,1)} %stack.9), calls=%async_computation | async-start | bytes 1048576 | tf_op jit(solution)/shard_map/all_to_all | solution.py:103
  172.4 86.9 %all-reduce.9.cloned.1.call-start = ((), (), s32[]{:S(2)}) async-start(), calls=%async_computation.6 | async-start | bytes 262144 | tf_op jit(solution)/shard_map/psum | solution.py:13
  172.4 18.7 %copy-start = (bf16[4,512,512]{2,1,0:T(8,128)(2,1)S(1)}, bf16[4,512,512]{2,1,0:T(8,128)(2,1)}, u32[]{:S(2)}) copy-start(bf16[4,512,512]{2,1,0:T(8,128)(2,1)} %param.8) | copy-start | bytes 6291460
  191.1 149.4 %all-reduce.11.cloned.1.call-start = ((), (), s32[]{:S(2)}) async-start(), calls=%async_computation.7 | async-start | bytes 524288 | tf_op jit(solution)/shard_map/psum | solution.py:114
  193.5 266.4 %reduce-scatter.4.cloned.1.call-start = ((), (), s32[]{:S(2)}) async-start(), calls=%async_computation.8 | async-start | bytes 1081344 | tf_op jit(solution)/shard_map/reduce_scatter | solution.py:116
  262.0 80.6 %copy-start.5 = (s32[32]{0:T(128)S(1)}, s32[32]{0:T(128)}, u32[]{:S(2)}) copy-start(s32[32]{0:T(128)} %param.11) | copy-start | bytes 388
  341.5 1.0 copy-start.2
  342.5 305.3 %all-reduce.13.cloned.1.call-start = ((), (), s32[]{:S(2)}) async-start(), calls=%async_computation.9 | async-start | bytes 262144 | tf_op jit(solution)/shard_map/psum | solution.py:13
  579.0 149.8 %all-reduce.15.cloned.1.call-start = ((), (), s32[]{:S(2)}) async-start(), calls=%async_computation.10 | async-start | bytes 524288 | tf_op jit(solution)/shard_map/psum | solution.py:114
  581.5 266.6 %reduce-scatter.6.cloned.1.call-start = ((), (), s32[]{:S(2)}) async-start(), calls=%async_computation.11 | async-start | bytes 1081344 | tf_op jit(solution)/shard_map/reduce_scatter | solution.py:116
  729.8 1.0 copy-start.3
  730.9 305.2 %all-reduce.17.cloned.1.call-start = ((), (), s32[]{:S(2)}) async-start(), calls=%async_computation.12 | async-start | bytes 262144 | tf_op jit(solution)/shard_map/psum | solution.py:13
  967.2 150.0 %all-reduce.19.cloned.1.call-start = ((), (), s32[]{:S(2)}) async-start(), calls=%async_computation.13 | async-start | bytes 524288 | tf_op jit(solution)/shard_map/psum | solution.py:114
  969.7 267.0 %reduce-scatter.8.cloned.1.call-start = ((), (), s32[]{:S(2)}) async-start(), calls=%async_computation.14 | async-start | bytes 1081344 | tf_op jit(solution)/shard_map/reduce_scatter | solution.py:116
  1118.2 1.0 copy-start.1
Sparse Core Ops, SparseCore 0:
  191.2 68.0 all-reduce.8
  261.9 78.5 all-reduce.10
  344.6 115.3 reduce-scatter.3
  579.1 68.6 all-reduce.12
  650.3 78.5 all-reduce.14
  732.8 115.3 reduce-scatter.5
  967.3 68.6 all-reduce.16
  1038.6 78.5 all-reduce.18
  1121.3 115.3 reduce-scatter.7
